TPU v7x, 256 devices: a whole 4x4x8 slice. The times are simulated.
256 devices in a mesh: seq: 64 (over x, z_lo, y, core), mp: 4 (over z_hi).
Axes of the slice: x: 4, y: 4, z: 8 (z_hi: 4, z_lo: 2; z = z_hi * 2 + z_lo), core: 2. Of those that a mesh axis runs over, the one named last changes fastest.
Arguments:
- tokens: bfloat16 [8192, 4096], P('seq', 'mp'), may hold values from -6 to 6
- w_proj: bfloat16 [4096, 3, 2048], P('seq', None, 'mp'), may hold values from -0.09375 to 0.09375
- short_filter: float32 [3, 3, 2048], P(None, None, 'mp'), may hold values from -3.5 to 3.5
- long_filter: float32 [2048, 8192], P(('mp', 'seq')), may hold values from -0.0625 to 0.0625
- skip_gain: float32 [2048], P('mp'), may hold values from -4 to 4
Outputs:
- gated: bfloat16 [8192, 2048], P('seq', 'mp')
All inputs are finite; a program needn't handle non-finite values.
Results may differ from a plain program's by a relative error of at most 0.012.
Values may be sent and summed in bfloat16 or wider, within the bound.
No kernel may reach another device: no remote copies, remote signals or barrier semaphores. Data moves between devices by JAX's collectives and lax.ppermute only.
A program may use at most 64 MiB of HBM per device.

v0:
```python
import math
import jax
import jax.numpy as jnp
from jax import lax
from jax.sharding import PartitionSpec as P


def shifted(value, axis, steps):
    count = lax.axis_size(axis)
    leading, last = (max(0, -steps), min(count, count - steps))
    return lax.ppermute(value, axis, [(source, source + steps) for source in range(leading, last)])


def transform(real_part, imag_part, orient, filled):
    length = real_part.shape[-1]
    first = math.gcd(length, 64)
    highest = lax.Precision.HIGHEST
    if length <= 64 or first == 1:
        counter = jnp.arange(length, dtype=jnp.int32)
        angles = (
            2.0
            * math.pi
            / length
            * (counter[:, None] * counter[None, :] % length).astype(jnp.float32)
        )
        cosine = jnp.cos(angles)
        sine = jnp.sin(angles)
        new_real = jnp.dot(real_part, cosine, precision=highest) - orient * jnp.dot(
            imag_part, sine, precision=highest
        )
        new_imag = jnp.dot(imag_part, cosine, precision=highest) + orient * jnp.dot(
            real_part, sine, precision=highest
        )
        return (new_real, new_imag)
    second = length // first
    outer = real_part.shape[:-1]
    live = first
    if filled > 0 and filled % second == 0:
        live = filled // second
    real_grid = real_part.reshape(outer + (first, second))[..., :live, :]
    imag_grid = imag_part.reshape(outer + (first, second))[..., :live, :]
    counter = jnp.arange(first, dtype=jnp.int32)
    angles = (
        2.0 * math.pi / first * (counter[:, None] * counter[None, :] % first).astype(jnp.float32)
    )
    cosine = jnp.cos(angles)[:live]
    sine = jnp.sin(angles)[:live]
    section_real = jnp.einsum(
        "...ab,ak->...kb", real_grid, cosine, precision=highest
    ) - orient * jnp.einsum("...ab,ak->...kb", imag_grid, sine, precision=highest)
    section_imag = jnp.einsum(
        "...ab,ak->...kb", imag_grid, cosine, precision=highest
    ) + orient * jnp.einsum("...ab,ak->...kb", real_grid, sine, precision=highest)
    freq_rows = jnp.arange(first, dtype=jnp.int32)[:, None]
    time_cols = jnp.arange(second, dtype=jnp.int32)[None, :]
    twiddle = 2.0 * math.pi / length * (freq_rows * time_cols).astype(jnp.float32)
    twist_cos = jnp.cos(twiddle)
    twist_sin = jnp.sin(twiddle)
    turned_real = section_real * twist_cos - orient * section_imag * twist_sin
    turned_imag = section_imag * twist_cos + orient * section_real * twist_sin
    inner_real, inner_imag = transform(turned_real, turned_imag, orient, 0)
    final_real = jnp.swapaxes(inner_real, -1, -2).reshape(outer + (length,))
    final_imag = jnp.swapaxes(inner_imag, -1, -2).reshape(outer + (length,))
    return (final_real, final_imag)


def mirrored(values):
    return jnp.concatenate([values[:, :1], values[:, :0:-1]], axis=1)


def long_conv(signal, kernel):
    seq_len = signal.shape[-1]
    padded_signal = jnp.pad(signal.astype(jnp.float32), ((0, 0), (0, seq_len)))
    padded_kernel = jnp.pad(kernel, ((0, 0), (0, seq_len)))
    joint_real, joint_imag = transform(padded_signal, padded_kernel, -1.0, seq_len)
    mirror_real = mirrored(joint_real)
    mirror_imag = mirrored(joint_imag)
    signal_real = 0.5 * (joint_real + mirror_real)
    signal_imag = 0.5 * (joint_imag - mirror_imag)
    kernel_real = 0.5 * (joint_imag + mirror_imag)
    kernel_imag = -0.5 * (joint_real - mirror_real)
    prod_real = signal_real * kernel_real - signal_imag * kernel_imag
    prod_imag = signal_real * kernel_imag + signal_imag * kernel_real
    back_real, back_imag = transform(prod_real, prod_imag, 1.0, 0)
    return back_real[:, :seq_len] / (2.0 * seq_len)


def on_device(tokens, w_proj, short_filter, long_filter, skip_gain):
    rows_dev = tokens.shape[0]
    margin = short_filter.shape[1] - 1
    width = w_proj.shape[2]
    source = lax.all_gather(tokens, "mp", axis=1, tiled=True)
    projected = jnp.einsum(
        "td,dpc->tpc",
        source,
        lax.all_gather(w_proj, "seq", axis=0, tiled=True),
        preferred_element_type=jnp.float32,
    ).astype(jnp.bfloat16)
    tail = shifted(projected[rows_dev - margin :], "seq", 1)
    extended = jnp.concatenate([tail, projected], axis=0).astype(jnp.float32)
    mixed = jnp.zeros((rows_dev, 3, width), jnp.float32)
    for offset in range(margin + 1):
        mixed = (
            mixed
            + short_filter[:, offset, :][None]
            * extended[margin - offset : margin - offset + rows_dev]
        )
    query_rows = mixed[:, 0]
    product = (mixed[:, 1] * mixed[:, 2]).astype(jnp.bfloat16)
    groups = lax.axis_size("seq")
    channel_count = width // groups
    outgoing = product.reshape(rows_dev, groups, channel_count).transpose(1, 2, 0)
    arrived = lax.all_to_all(outgoing, "seq", split_axis=0, concat_axis=2, tiled=True)[0]
    convolved = long_conv(arrived, long_filter).astype(jnp.bfloat16)[None]
    returned = lax.all_to_all(convolved, "seq", split_axis=2, concat_axis=0, tiled=True)
    back_rows = returned.transpose(2, 0, 1).reshape(rows_dev, width)
    result = query_rows * (
        back_rows.astype(jnp.float32) + skip_gain[None, :] * product.astype(jnp.float32)
    )
    return result.astype(jnp.bfloat16)


def solution(mesh):
    return jax.shard_map(
        on_device,
        mesh=mesh,
        in_specs=(
            P("seq", "mp"),
            P("seq", None, "mp"),
            P(None, None, "mp"),
            P(("mp", "seq"), None),
            P("mp"),
        ),
        out_specs=P("seq", "mp"),
        check_vma=False,
    )
```

profile of v0, /device:TPU:1, one launch (start us, length us, event | category | flops | bytes accessed | tf_op | source)
XLA Modules:
  0.0 374.8 jit_solution(6726618726081883636)
XLA Ops:
  9.7 37.3 %all-gather.3.cloned.1.call-done = bf16[128,4096]{1,0:T(8,128)(2,1)} async-done(((bf16[128,1024]{1,0:T(8,128)(2,1)}), bf16[128,4096]{1,0:T(8,128)(2,1)}) %all-gather.3.cloned.1.call-update) | async-done | bytes 1048592 | tf_op jit(solution)/shard_map/all_gather | solution.py:92
  47.0 120.2 %all-gather.5.cloned.1.call-done = bf16[4096,3,512]{2,0,1:T(8,128)(2,1)} async-done(((bf16[64,3,512]{2,0,1:T(8,128)(2,1)}), bf16[4096,3,512]{2,0,1:T(8,128)(2,1)}) %all-gather.5.cloned.1.call-update) | async-done | bytes 12582928 | tf_op jit(solution)/shard_map/all_gather | solution.py:96
  167.2 6.7 %convolution_convert_fusion = bf16[128,3,512]{2,0,1:T(8,128)(2,1)S(1)} fusion(bf16[4096,3,512]{2,0,1:T(8,128)(2,1)} %all-gather.5.cloned.1.call-done, bf16[128,4096]{1,0:T(8,128)(2,1)} %all-gather.3.cloned.1.call-done), kind=kOutput, calls=%fused_computation.14 | convolution fusion | flops 1610809344 | bytes 14024704 | tf_op jit(solution)/shard_map/td,dpc->tpc/dot_general | solution.py:93
  173.9 2.8 collective-permute-start
  179.5 8.7 %all-to-all-start = ((bf16[64,8,128]{2,1,0:T(8,128)(2,1)}), bf16[64,8,128]{2,1,0:T(8,128)(2,1)S(1)}, u32[]{:S(2)}, u32[]{:S(2)}) async-start(bf16[64,8,128]{2,1,0:T(8,128)(2,1)} %bitcast.7), calls=%async_computation | async-start | bytes 262144 | tf_op jit(solution)/shard_map/all_to_all | solution.py:113
  189.1 7.4 %all-to-all-done = bf16[64,8,128]{2,1,0:T(8,128)(2,1)S(1)} async-done(((bf16[64,8,128]{2,1,0:T(8,128)(2,1)}), bf16[64,8,128]{2,1,0:T(8,128)(2,1)S(1)}, u32[]{:S(2)}, u32[]{:S(2)}) %all-to-all-start) | async-done | bytes 131104 | tf_op jit(solution)/shard_map/all_to_all | solution.py:113
  199.3 3.3 fusion.41
  205.7 3.3 fusion.43
  209.0 3.3 fusion.5
  212.3 4.7 %add_bitcast_fusion.1 = (f32[8,64,64,4]{1,2,3,0:T(8,128)}, f32[8,64,64,4]{1,2,3,0:T(8,128)S(1)}) fusion(f32[64,8,64,4]{2,0,3,1:T(8,128)S(1)} %fusion.5, f32[64,4]{0,1:T(4,128)S(1)} %get-tuple-element.23, f32[64,4]{0,1:T(4,128)S(1)} %get-tuple-element.22, f32[64,8,64,4]{2,0,3,1:T(8,128)S(1)} %fusion.43, f32[8,64,64,4]{2,1,3,0:T(8,128)S(1)} %copy.114), kind=kOutput, calls=%fused_computation.24 | convolution fusion | flops 101769216 | bytes 2623488 | tf_op jit(solution)/shard_map/...ab,ak->...kb/dot_general | solution.py:50
  220.9 3.1 fusion.4
  231.0 2.1 fusion.2
  234.4 8.9 %reverse = f32[8,16384]{1,0:T(8,128)S(1)} reverse(f32[8,16384]{1,0:T(8,128)S(1)} %bitcast.226), dimensions={1} | reverse | bytes 1048576
  243.5 9.3 %reverse.1 = f32[8,16384]{1,0:T(8,128)S(1)} reverse(f32[8,16384]{1,0:T(8,128)S(1)} %bitcast.229), dimensions={1} | reverse | bytes 1048576
  258.1 3.3 fusion.39
  264.5 3.3 fusion.45
  267.8 3.3 convolution_add_fusion
  271.1 4.6 %add_bitcast_fusion = (f32[8,64,64,4]{1,2,3,0:T(8,128)S(1)}, f32[8,64,64,4]{1,2,3,0:T(8,128)}) fusion(f32[64,8,64,4]{2,0,3,1:T(8,128)S(1)} %convolution_add_fusion, f32[64,4]{0,1:T(4,128)S(1)} %fusion.76, f32[64,4]{0,1:T(4,128)S(1)} %get-tuple-element.22, f32[64,8,64,4]{2,0,3,1:T(8,128)S(1)} %fusion.45, f32[8,64,64,4]{2,1,3,0:T(8,128)S(1)} %copy.134), kind=kOutput, calls=%fused_computation.22 | convolution fusion | flops 101638144 | bytes 2623488 | tf_op jit(solution)/shard_map/...ab,ak->...kb/dot_general | solution.py:50
  282.4 6.8 %copy.142 = bf16[1,8,8192]{1,0,2:T(2,128)(2,1)} copy(bf16[1,8,8192]{2,1,0:T(8,128)(2,1)S(1)} %fusion.21) | data formatting | bytes 262144 | tf_op jit(solution)/shard_map/broadcast_in_dim | solution.py:114
  289.7 45.4 %reduce = bf16[8192,8]{1,0:T(8,128)(2,1)S(1)} reduce(bf16[8192,1,8]{2,1,0:T(2,128)(2,1)} %bitcast.215, bf16[]{:T(256)} %broadcast.303), dimensions={1}, to_apply=%bitcast.180.reduce_sub_computation | reduce | bytes 262146
  335.1 2.3 reshape.159
  337.4 12.7 %all_to_all.21 = bf16[64,2,512]{2,1,0:T(2,128)(2,1)S(1)} all-to-all(bf16[64,2,512]{2,1,0:T(2,128)(2,1)S(1)} %reshape.159), channel_id=1, replica_groups=mesh['seq'=64,'mp'=4] {'seq'}, dimensions={0} | all-to-all | bytes 262144 | tf_op jit(solution)/shard_map/all_to_all | solution.py:115
  350.1 8.7 %reshape.160 = bf16[8192,1,8]{2,1,0:T(2,128)(2,1)} reshape(bf16[64,2,512]{2,1,0:T(2,128)(2,1)S(1)} %all_to_all.21) | data formatting | bytes 262144
  358.8 7.8 %copy.143 = bf16[1,8,8192]{2,1,0:T(8,128)(2,1)S(1)} copy(bf16[1,8,8192]{1,0,2:T(2,128)(2,1)} %bitcast.216) | data formatting | bytes 262144 | tf_op jit(solution)/shard_map/all_to_all | solution.py:115
  (82 shorter events, 41.7 us)
Async XLA Ops:
  6.5 181.7 %copy-start.3 = (f32[8,8192]{1,0:T(8,128)S(1)}, f32[8,8192]{1,0:T(8,128)}, u32[]{:S(2)}) copy-start(f32[8,8192]{1,0:T(8,128)} %param.8) | copy-start | bytes 786436
  6.5 40.4 %all-gather.3.cloned.1.call-start = ((), (), s32[]{:S(2)}) async-start(), calls=%async_computation.2 | async-start | bytes 1310720 | tf_op jit(solution)/shard_map/all_gather | solution.py:92
  7.3 159.9 %all-gather.5.cloned.1.call-start = ((), (), s32[]{:S(2)}) async-start(), calls=%async_computation.3 | async-start | bytes 12779520 | tf_op jit(solution)/shard_map/all_gather | solution.py:96
  173.9 3.6 collective-permute-start
  177.8 0.9 copy-start
  179.5 17.0 %all-to-all-start = ((bf16[64,8,128]{2,1,0:T(8,128)(2,1)}), bf16[64,8,128]{2,1,0:T(8,128)(2,1)S(1)}, u32[]{:S(2)}, u32[]{:S(2)}) async-start(bf16[64,8,128]{2,1,0:T(8,128)(2,1)} %bitcast.7), calls=%async_computation | async-start | bytes 262144 | tf_op jit(solution)/shard_map/all_to_all | solution.py:113
  227.8 25.2 %slice-start = ((f32[8,16384]{1,0:T(8,128)}), f32[8,1]{1,0:T(8,128)S(1)}, s32[]{:S(2)}) async-start(f32[8,16384]{1,0:T(8,128)} %reshape.130), calls=%async_computation.4 | async-start | bytes 8192 | tf_op jit(solution)/shard_map/slice | solution.py:68
  227.8 25.6 %copy-start.2 = (f32[8,64,256]{2,1,0:T(8,128)S(1)}, f32[8,64,256]{2,1,0:T(8,128)}, u32[]{:S(2)}) copy-start(f32[8,64,256]{2,1,0:T(8,128)} %reshape.129) | copy-start | bytes 1572868
  282.0 85.0 %copy-start.1 = (f32[128,3,512]{2,0,1:T(8,128)S(1)}, f32[128,3,512]{2,0,1:T(8,128)}, u32[]{:S(2)}) copy-start(f32[128,3,512]{2,0,1:T(8,128)} %copy-done) | copy-start | bytes 2359300
  282.0 85.0 %copy-start.4 = (f32[512]{0:T(512)S(1)}, f32[512]{0:T(512)}, u32[]{:S(2)}) copy-start(f32[512]{0:T(512)} %param.9) | copy-start | bytes 6148
Sparse Core Ops, SparseCore 0:
  9.1 37.7 all-gather.2
  48.8 118.2 all-gather.4
where the time goes:
time: 379 us; the launch traced here: 375 us
  waiting for transfers between devices  167 us (44%)
  local copies, waits for them, and re-layouts  67.2 us (18%)
  matrix products  54 us (14%)
  other arithmetic  48.3 us (13%)
  between operations  14.1 us (4%)
  blocking collectives  12.7 us (3%)
  starting transfers between devices  11.5 us (3%)
    all_gather x1, waiting for transfers between devices, on_device(): lax.all_gather(w_proj, 'seq', axis=0, tiled=True)  120 us
    unnamed x2, other arithmetic  45.4 us
    all_gather x1, waiting for transfers between devices, on_device(): source = lax.all_gather(tokens, 'mp', axis=1, tiled=True)  37.3 us
    unnamed x22, local copies, waits for them, and re-layouts  31.3 us
    all_to_all x1, blocking collectives, on_device(): lax.all_to_all(convolved, 'seq', split_axis=2, concat_axis=0, tiled=True)  12.7 us
    dot_general x4, matrix products, transform(): jnp.einsum('...ab,ak->...kb', imag_grid, sine, precision=highest)  10.8 us
    all_to_all x1, starting transfers between devices, on_device(): lax.all_to_all(outgoing, 'seq', split_axis=0, concat_axis=2, tiled=True)[0]  8.66 us
    dot_general x4, matrix products, transform(): jnp.einsum('...ab,ak->...kb', imag_grid, cosine, precision=highest)  7.92 us
  transfers between devices with their start and end apart: 4, of which 4 were waited for; matrix products, arithmetic and copies ran while one was open for 1% of the time, Pallas kernels for 0%

commit v1 on v0

--- a/solution.py
+++ b/solution.py
@@ -112,7 +112,9 @@
     outgoing = product.reshape(rows_dev, groups, channel_count).transpose(1, 2, 0)
     arrived = lax.all_to_all(outgoing, "seq", split_axis=0, concat_axis=2, tiled=True)[0]
     convolved = long_conv(arrived, long_filter).astype(jnp.bfloat16)[None]
-    returned = lax.all_to_all(convolved, "seq", split_axis=2, concat_axis=0, tiled=True)
+    pieces = jnp.split(convolved, lax.axis_size("seq"), axis=2)
+    received = lax.all_to_all(jnp.stack(pieces), "seq", 0, 0)
+    returned = jnp.concatenate(received, axis=0)
     back_rows = returned.transpose(2, 0, 1).reshape(rows_dev, width)
     result = query_rows * (
         back_rows.astype(jnp.float32) + skip_gain[None, :] * product.astype(jnp.float32)

time: 379 us -> 355 us (0.937)
  other arithmetic: 48.3 us -> 2.9 us
  local copies, waits for them, and re-layouts: 67.2 us -> 79.6 us
  matrix products: 54 us -> 60.9 us
    unnamed x2 -> x0, other arithmetic: 45.4 us -> none
    unnamed x22 -> x77, local copies, waits for them, and re-layouts: 31.3 us -> 58.2 us
    all_to_all x1 -> x0, local copies, waits for them, and re-layouts: 7.79 us -> none  [on_device(): lax.all_to_all(convolved, 'seq', split_axis=2, concat_axis=0, tiled=True)]
    broadcast_in_dim x1 -> x0, local copies, waits for them, and re-layouts: 6.75 us -> none  [on_device(): convolved = long_conv(arrived, long_filter).astype(jnp.bfloat16)[None]]
where the time goes in v1:
time: 355 us; the launch traced here: 349 us
  waiting for transfers between devices  167 us (47%)
  local copies, waits for them, and re-layouts  79.6 us (22%)
  matrix products  60.9 us (17%)
  between operations  14.2 us (4%)
  blocking collectives  12.7 us (4%)
  starting transfers between devices  11.5 us (3%)
    all_gather x1, waiting for transfers between devices, on_device(): lax.all_gather(w_proj, 'seq', axis=0, tiled=True)  120 us
    unnamed x77, local copies, waits for them, and re-layouts  58.2 us
    all_gather x1, waiting for transfers between devices, on_device(): source = lax.all_gather(tokens, 'mp', axis=1, tiled=True)  37.3 us
    dot_general x4, matrix products, transform(): jnp.einsum('...ab,ak->...kb', imag_grid, sine, precision=highest)  13.4 us
    all_to_all x1, blocking collectives, on_device(): received = lax.all_to_all(jnp.stack(pieces), 'seq', 0, 0)  12.7 us
    dot_general x4, matrix products, transform(): jnp.einsum('...ab,ak->...kb', real_grid, cosine, precision=highest)  9.83 us
    all_to_all x1, starting transfers between devices, on_device(): lax.all_to_all(outgoing, 'seq', split_axis=0, concat_axis=2, tiled=True)[0]  8.67 us
    dot_general x4, matrix products, transform(): jnp.einsum('...ab,ak->...kb', imag_grid, cosine, precision=highest)  7.92 us
  transfers between devices with their start and end apart: 4, of which 4 were waited for; matrix products, arithmetic and copies ran while one was open for 1% of the time, Pallas kernels for 0%

profile of v1, /device:TPU:1, one launch (start us, length us, event | category | flops | bytes accessed | tf_op | source)
XLA Modules:
  0.0 348.8 jit_solution(6762061076999726116)
XLA Ops:
  9.7 37.3 %all-gather.3.cloned.1.call-done = bf16[128,4096]{1,0:T(8,128)(2,1)} async-done(((bf16[128,1024]{1,0:T(8,128)(2,1)}), bf16[128,4096]{1,0:T(8,128)(2,1)}) %all-gather.3.cloned.1.call-update) | async-done | bytes 1048592 | tf_op jit(solution)/shard_map/all_gather | solution.py:92
  47.0 120.2 %all-gather.5.cloned.1.call-done = bf16[4096,3,512]{2,0,1:T(8,128)(2,1)} async-done(((bf16[64,3,512]{2,0,1:T(8,128)(2,1)}), bf16[4096,3,512]{2,0,1:T(8,128)(2,1)}) %all-gather.5.cloned.1.call-update) | async-done | bytes 12582928 | tf_op jit(solution)/shard_map/all_gather | solution.py:96
  167.2 6.7 %convolution_convert_fusion = bf16[128,3,512]{2,0,1:T(8,128)(2,1)S(1)} fusion(bf16[4096,3,512]{2,0,1:T(8,128)(2,1)} %all-gather.5.cloned.1.call-done, bf16[128,4096]{1,0:T(8,128)(2,1)} %all-gather.3.cloned.1.call-done), kind=kOutput, calls=%fused_computation.14 | convolution fusion | flops 1610809344 | bytes 14024704 | tf_op jit(solution)/shard_map/td,dpc->tpc/dot_general | solution.py:93
  173.9 2.8 collective-permute-start
  178.7 8.7 %all-to-all-start = ((bf16[64,8,128]{2,1,0:T(8,128)(2,1)}), bf16[64,8,128]{2,1,0:T(8,128)(2,1)S(1)}, u32[]{:S(2)}, u32[]{:S(2)}) async-start(bf16[64,8,128]{2,1,0:T(8,128)(2,1)} %bitcast.7), calls=%async_computation | async-start | bytes 262144 | tf_op jit(solution)/shard_map/all_to_all | solution.py:113
  188.2 7.4 %all-to-all-done = bf16[64,8,128]{2,1,0:T(8,128)(2,1)S(1)} async-done(((bf16[64,8,128]{2,1,0:T(8,128)(2,1)}), bf16[64,8,128]{2,1,0:T(8,128)(2,1)S(1)}, u32[]{:S(2)}, u32[]{:S(2)}) %all-to-all-start) | async-done | bytes 131104 | tf_op jit(solution)/shard_map/all_to_all | solution.py:113
  198.4 4.3 %fusion.43 = f32[64,8,64,4]{2,0,3,1:T(8,128)} fusion(f32[8,64,64,4]{2,1,3,0:T(8,128)S(1)} %copy.136), kind=kOutput, calls=%fused_computation.152 | convolution fusion | flops 100720640 | bytes 1048576 | tf_op jit(solution)/shard_map/...ab,ak->...kb/dot_general | solution.py:48
  204.0 1.8 copy.139
  205.8 3.3 fusion.41
  209.1 3.3 fusion.5
  212.3 5.8 %add_bitcast_fusion.1 = (f32[8,64,64,4]{1,2,3,0:T(8,128)S(1)}, f32[8,64,64,4]{1,2,3,0:T(8,128)}) fusion(f32[64,8,64,4]{2,0,3,1:T(8,128)S(1)} %fusion.5, f32[64,4]{0,1:T(4,128)S(1)} %get-tuple-element.23, f32[64,4]{0,1:T(4,128)S(1)} %get-tuple-element.22, f32[64,8,64,4]{2,0,3,1:T(8,128)} %fusion.43, f32[8,64,64,4]{2,1,3,0:T(8,128)S(1)} %copy.139), kind=kOutput, calls=%fused_computation.24 | convolution fusion | flops 101769216 | bytes 2623488 | tf_op jit(solution)/shard_map/...ab,ak->...kb/dot_general | solution.py:50
  220.2 1.9 fusion.74
  222.1 2.9 fusion.72
  225.1 3.1 fusion.4
  232.2 3.3 fusion.2
  236.8 47.7 %reverse = f32[8,16384]{1,0:T(8,128)S(1)} reverse(f32[8,16384]{1,0:T(8,128)} %bitcast.469), dimensions={1} | reverse | bytes 1048576
  284.7 9.3 %reverse.1 = f32[8,16384]{1,0:T(8,128)S(1)} reverse(f32[8,16384]{1,0:T(8,128)S(1)} %bitcast.470), dimensions={1} | reverse | bytes 1048576
  299.3 4.3 %fusion.45 = f32[64,8,64,4]{2,0,3,1:T(8,128)} fusion(f32[8,64,64,4]{2,1,3,0:T(8,128)S(1)} %copy.156), kind=kOutput, calls=%fused_computation.154 | convolution fusion | flops 100720640 | bytes 1048576 | tf_op jit(solution)/shard_map/...ab,ak->...kb/dot_general | solution.py:48
  306.7 3.3 fusion.39
  310.0 3.3 convolution_add_fusion
  313.3 6.1 %add_bitcast_fusion = (f32[8,64,64,4]{1,2,3,0:T(8,128)}, f32[8,64,64,4]{1,2,3,0:T(8,128)}) fusion(f32[64,8,64,4]{2,0,3,1:T(8,128)S(1)} %convolution_add_fusion, f32[64,4]{0,1:T(4,128)S(1)} %fusion.76, f32[64,4]{0,1:T(4,128)S(1)} %get-tuple-element.22, f32[64,8,64,4]{2,0,3,1:T(8,128)} %fusion.45, f32[8,64,64,4]{2,1,3,0:T(8,128)S(1)} %copy.159), kind=kOutput, calls=%fused_computation.22 | convolution fusion | flops 101638144 | bytes 2623488 | tf_op jit(solution)/shard_map/...ab,ak->...kb/dot_general | solution.py:50
  322.7 1.9 fusion.70
  324.6 2.1 fusion
  328.2 12.7 %all_to_all.14 = bf16[64,1,8,128]{3,2,1,0:T(8,128)(2,1)S(1)} all-to-all(bf16[64,1,8,128]{3,2,1,0:T(8,128)(2,1)S(1)} %constant_dynamic-update-slice_fusion), channel_id=1, replica_groups=mesh['seq'=64,'mp'=4] {'seq'}, dimensions={0} | all-to-all | bytes 262144 | tf_op jit(solution)/shard_map/all_to_all | solution.py:116
  (133 shorter events, 31.2 us)
Async XLA Ops:
  6.5 180.8 %copy-start.1 = (f32[8,8192]{1,0:T(8,128)S(1)}, f32[8,8192]{1,0:T(8,128)}, u32[]{:S(2)}) copy-start(f32[8,8192]{1,0:T(8,128)} %param.8) | copy-start | bytes 786436
  6.5 40.4 %all-gather.3.cloned.1.call-start = ((), (), s32[]{:S(2)}) async-start(), calls=%async_computation.2 | async-start | bytes 1310720 | tf_op jit(solution)/shard_map/all_gather | solution.py:92
  7.3 159.9 %all-gather.5.cloned.1.call-start = ((), (), s32[]{:S(2)}) async-start(), calls=%async_computation.3 | async-start | bytes 12779520 | tf_op jit(solution)/shard_map/all_gather | solution.py:96
  173.9 3.6 %collective-permute-start = (bf16[2,3,512]{2,0,1:T(2,128)(2,1)S(1)}, bf16[2,3,512]{2,0,1:T(2,128)(2,1)S(1)}, u32[]{:S(2)}, u32[]{:S(2)}) collective-permute-start(bf16[2,3,512]{2,0,1:T(2,128)(2,1)S(1)} %slice.84), channel_id=1, source_target_pairs={{0,4},{4,8},{8,12},{12,16},{16,20},{20,24},{24,28},{28,32},{32,36}... | collective-permute-start | bytes 18440 | tf_op jit(solution)/shard_map/ppermute | solution.py:11
  178.7 17.0 %all-to-all-start = ((bf16[64,8,128]{2,1,0:T(8,128)(2,1)}), bf16[64,8,128]{2,1,0:T(8,128)(2,1)S(1)}, u32[]{:S(2)}, u32[]{:S(2)}) async-start(bf16[64,8,128]{2,1,0:T(8,128)(2,1)} %bitcast.7), calls=%async_computation | async-start | bytes 262144 | tf_op jit(solution)/shard_map/all_to_all | solution.py:113
  232.2 62.4 %copy-start = (f32[8,64,256]{2,1,0:T(8,128)S(1)}, f32[8,64,256]{2,1,0:T(8,128)}, u32[]{:S(2)}) copy-start(f32[8,64,256]{2,1,0:T(8,128)} %reshape.130) | copy-start | bytes 1572868
  306.7 34.3 %copy-start.2 = (f32[512]{0:T(512)S(1)}, f32[512]{0:T(512)}, u32[]{:S(2)}) copy-start(f32[512]{0:T(512)} %param.9) | copy-start | bytes 6148
Sparse Core Ops, SparseCore 0:
  9.1 37.7 all-gather.2
  48.8 118.2 all-gather.4
